TPU v7x, 512 devices: a whole 4x8x8 slice. The times are simulated.
512 devices in a mesh: req: 64 (over z, x, core), voc: 8 (over y).
Axes of the slice: x: 4, y: 8, z: 8, core: 2. Of those that a mesh axis runs over, the one named last changes fastest.
Arguments:
- hidden: bfloat16 [65536, 1600], P(('req', 'voc')), may hold values from -60 to 60
- norm_gain: float32 [1600], replicated, may hold values from 0.25 to 1.75
- unembed: bfloat16 [16384, 1600], P(('req', 'voc')), may hold values from -2 to 2
- targets: int32 [65536], P(('req', 'voc')), may hold values from 0 to 16383
- live: int32 [65536], P(('req', 'voc')), may hold values from 0 to 1, as said below
Outputs:
- logprob: float32 [65536], P(('req', 'voc'))
- entropy: float32 [65536], P(('req', 'voc'))
Inputs may be any that keep to these rules, and one draw needn't show every extreme that they name: Within each aligned block of 1024 slots (one owner's) the live slots form a prefix of 128 to 1024 slots, and in every draw at least one block is wholly live.
All inputs are finite; a program needn't handle non-finite values.
Results may differ from a plain program's by a relative error of at most 0.0067.
Values may be sent and summed in bfloat16 or wider, within the bound.
No kernel may reach another device: no remote copies, remote signals or barrier semaphores. Data moves between devices by JAX's collectives and lax.ppermute only.
A program may use at most 64 MiB of HBM per device.

v0:
```python
import jax
import jax.numpy as jnp
from jax import lax
from jax.sharding import PartitionSpec as P


def merged_2(value, axis, join):
    pieces = jax.tree.map(lambda part: lax.all_gather(part, axis), value)
    head = jax.tree.map(lambda part: part[0], pieces)
    tail = jax.tree.map(lambda part: part[1:], pieces)
    so_far, _ = lax.scan(lambda so_far, piece: (join(so_far, piece), None), head, tail)
    return so_far


def combine_stats(first, second):
    top = jnp.maximum(first[0], second[0])
    scale_one = jnp.exp(first[0] - top)
    scale_two = jnp.exp(second[0] - top)
    total = first[1] * scale_one + second[1] * scale_two
    spread = scale_one * (first[2] + (first[0] - top) * first[1]) + scale_two * (
        second[2] + (second[0] - top) * second[1]
    )
    return (top, total, spread, first[3] + second[3])


def on_device(hidden, norm_gain, unembed, targets, live):
    rows, wanted = (
        lax.all_gather(hidden, "voc", axis=0, tiled=True),
        lax.all_gather(targets, "voc", axis=0, tiled=True),
    )
    wide = rows.astype(jnp.float32)
    normed = (
        wide * lax.rsqrt(jnp.mean(wide * wide, axis=1, keepdims=True) + 1e-06) * norm_gain
    ).astype(jnp.bfloat16)
    groups = lax.axis_size("voc")
    column = lax.axis_index("voc")
    width = unembed.shape[0]
    count = normed.shape[0]
    zeros = jnp.zeros((count,), jnp.float32)
    start_carry = (jnp.full((count,), -1e30, jnp.float32), zeros, zeros, zeros)
    whole = lax.all_gather(unembed, "req", axis=0, tiled=True)
    stats = start_carry
    step = min(512, whole.shape[0])
    for first in range(0, whole.shape[0], step):
        piece = whole[first : first + step]
        logits = lax.dot_general(
            normed, piece, (((1,), (1,)), ((), ())), preferred_element_type=jnp.float32
        )
        local = first + jnp.arange(piece.shape[0], dtype=jnp.int32)
        vocab_ids = local // width * (groups * width) + column * width + local % width
        chosen = jnp.sum(jnp.where(vocab_ids[None, :] == wanted[:, None], logits, 0.0), axis=1)
        fold_top = jnp.max(logits, axis=1)
        shifted = logits - fold_top[:, None]
        weights = jnp.exp(shifted)
        newer = (fold_top, jnp.sum(weights, axis=1), jnp.sum(weights * shifted, axis=1), chosen)
        stats = combine_stats(stats, newer)
    mine = count // groups
    merged = merged_2(stats, "voc", combine_stats)
    top = lax.dynamic_slice_in_dim(merged[0], column * mine, mine)
    total = lax.dynamic_slice_in_dim(merged[1], column * mine, mine)
    spread = lax.dynamic_slice_in_dim(merged[2], column * mine, mine)
    picked = lax.dynamic_slice_in_dim(merged[3], column * mine, mine)
    mask = live.astype(jnp.float32)
    logprob = (picked - top - jnp.log(total)) * mask
    entropy = (jnp.log(total) - spread / total) * mask
    return (logprob, entropy)


def solution(mesh):
    return jax.shard_map(
        on_device,
        mesh=mesh,
        in_specs=(
            P(("req", "voc"), None),
            P(),
            P(("req", "voc"), None),
            P(("req", "voc")),
            P(("req", "voc")),
        ),
        out_specs=(P(("req", "voc")), P(("req", "voc"))),
        check_vma=False,
    )
```

profile of v0, /device:TPU:16, one launch (start us, length us, event | category | flops | bytes accessed | tf_op | source)
XLA Modules:
  0.0 284.1 jit_solution(10954525450019727820)
XLA Ops:
  7.2 0.0 copy-start.3
  7.2 0.0 all-gather.8.cloned.1.call-start
  7.2 0.7 all-gather.8.cloned.1.call-update
  7.9 0.0 all-gather.10.cloned.1.call-start
  8.0 0.7 all-gather.10.cloned.1.call-update
  8.7 16.5 %all-gather.4 = s32[8,1,128]{2,1,0:T(1,128)S(1)} all-gather(s32[1,1,128]{2,1,0:T(1,128)} %bitcast.74), channel_id=1, replica_groups=mesh['req'=64,'voc'=8] {'voc'}, dimensions={0}, use_global_device_ids=true | all-gather | bytes 4608 | tf_op jit(solution)/shard_map/all_gather | solution.py:29
  25.1 46.9 %all-gather.8.cloned.1.call-done = bf16[1024,1600]{0,1:T(8,128)(2,1)} async-done(((bf16[128,1600]{0,1:T(8,128)(2,1)}), bf16[1024,1600]{0,1:T(8,128)(2,1)}) %all-gather.8.cloned.1.call-update) | async-done | bytes 3276816 | tf_op jit(solution)/shard_map/all_gather | solution.py:28
  72.1 2.8 fusion
  74.9 87.4 %all-gather.10.cloned.1.call-done = bf16[2048,1600]{1,0:T(8,128)(2,1)} async-done(((bf16[32,1600]{1,0:T(8,128)(2,1)}), bf16[2048,1600]{1,0:T(8,128)(2,1)}) %all-gather.10.cloned.1.call-update) | async-done | bytes 6553616 | tf_op jit(solution)/shard_map/all_gather | solution.py:41
  162.3 0.0 copy-done.3
  162.3 3.8 %fusion.44 = (f32[1024]{0:T(1024)S(1)}, f32[1024,512]{0,1:T(8,128)S(1)}) fusion(bf16[1024,1600]{0,1:T(8,128)(2,1)S(1)} %copy-done, f32[1600]{0:T(1024)S(1)} %copy-done.3, f32[1024]{0:T(1024)S(1)} %add_rsqrt_fusion, bf16[2048,1600]{1,0:T(8,128)(2,1)} %all-gather.10.cloned.1.call-done), kind=kOutput, calls=%fused_computation.103 | convolution fusion | flops 1684798464 | bytes 7092480 | tf_op jit(solution)/shard_map/dot_general | solution.py:46
  166.2 2.2 fusion.45
  168.4 2.2 fusion.46
  170.7 2.2 fusion.47
  172.9 0.0 copy-start.1
  173.0 3.9 %fusion.3 = (f32[1024]{0:T(1024)S(1)}, f32[1024]{0:T(1024)S(1)}, f32[1024]{0:T(1024)S(1)}, f32[1024]{0:T(1024)S(1)}, f32[1024]{0:T(1024)S(1)}, /*index=5*/f32[10...) fusion(f32[1024,512]{0,1:T(8,128)S(1)} %get-tuple-element.108, ...), kind=kLoop, calls=%fused_computation.19 | loop fusion | flops 14667776 | bytes 8466432 | tf_op jit(solution)/shard_map/reduce_sum | solution.py:55
  176.9 25.4 %all-gather = f32[8192]{0:T(1024)S(1)} all-gather(f32[1024]{0:T(1024)S(1)} %add_add_fusion), channel_id=2, replica_groups=mesh['req'=64,'voc'=8] {'voc'}, dimensions={0}, use_global_device_ids=true | all-gather | bytes 36864 | tf_op jit(solution)/shard_map/all_gather | solution.py:8
  202.3 0.1 add_bitcast_fusion
  202.4 24.5 %all-gather.2 = f32[8,1,1024]{2,1,0:T(1,128)S(1)} all-gather(f32[1,1,1024]{2,1,0:T(1,128)S(1)} %get-tuple-element.94), channel_id=1, replica_groups=mesh['req'=64,'voc'=8] {'voc'}, dimensions={0}, use_global_device_ids=true | all-gather | bytes 36864 | tf_op jit(solution)/shard_map/all_gather | solution.py:8
  226.9 24.5 %all-gather.1 = f32[8,1,1024]{2,1,0:T(1,128)S(1)} all-gather(f32[1,1,1024]{2,1,0:T(1,128)S(1)} %get-tuple-element.95), channel_id=1, replica_groups=mesh['req'=64,'voc'=8] {'voc'}, dimensions={0}, use_global_device_ids=true | all-gather | bytes 36864 | tf_op jit(solution)/shard_map/all_gather | solution.py:8
  251.3 24.5 %all-gather.3 = f32[8,1,1024]{2,1,0:T(1,128)S(1)} all-gather(f32[1,1,1024]{2,1,0:T(1,128)S(1)} %get-tuple-element.88), channel_id=1, replica_groups=mesh['req'=64,'voc'=8] {'voc'}, dimensions={0}, use_global_device_ids=true | all-gather | bytes 36864 | tf_op jit(solution)/shard_map/all_gather | solution.py:8
  275.8 0.8 while.16
  276.7 0.0 copy-done.1
  276.7 0.6 subtract_multiply_fusion
  (63 shorter events, 0.5 us)
Async XLA Ops:
  7.2 155.2 %copy-start.3 = (f32[1600]{0:T(1024)S(1)}, f32[1600]{0:T(1024)}, u32[]{:S(2)}) copy-start(f32[1600]{0:T(1024)} %param.8) | copy-start | bytes 19204
  7.2 64.9 %all-gather.8.cloned.1.call-start = ((), (), s32[]{:S(2)}) async-start(), calls=%async_computation | async-start | bytes 3686400 | tf_op jit(solution)/shard_map/all_gather | solution.py:28
  7.9 154.4 %all-gather.10.cloned.1.call-start = ((), (), s32[]{:S(2)}) async-start(), calls=%async_computation.1 | async-start | bytes 6922240 | tf_op jit(solution)/shard_map/all_gather | solution.py:41
  72.1 90.2 %copy-start = (bf16[1024,1600]{0,1:T(8,128)(2,1)S(1)}, bf16[1024,1600]{0,1:T(8,128)(2,1)}, u32[]{:S(2)}) copy-start(bf16[1024,1600]{0,1:T(8,128)(2,1)} %all-gather.8.cloned.1.call-done) | copy-start | bytes 9830404
  162.3 3.8 %copy-start.2 = (bf16[2048,1600]{1,0:T(8,128)(2,1)S(1)}, bf16[2048,1600]{1,0:T(8,128)(2,1)}, u32[]{:S(2)}) copy-start(bf16[2048,1600]{1,0:T(8,128)(2,1)} %all-gather.10.cloned.1.call-done) | copy-start | bytes 19660804
  172.9 103.7 %copy-start.1 = (s32[128]{0:T(128)S(1)}, s32[128]{0:T(128)}, u32[]{:S(2)}) copy-start(s32[128]{0:T(128)} %param.11) | copy-start | bytes 1540
Sparse Core Ops, SparseCore 0:
  10.0 62.0 all-gather.7
  75.4 86.8 all-gather.9
where the time goes:
time: 284 us
  waiting for transfers between devices  136 us (48%)
  blocking collectives  115 us (40%)
  between operations  14.2 us (5%)
  matrix products  10.6 us (4%)
  other arithmetic  7.67 us (3%)
    all_gather x4, blocking collectives, merged_2(): pieces = jax.tree.map(lambda part: lax.all_gather(part, axis), value)  98.8 us
    all_gather x1, waiting for transfers between devices, on_device(): whole = lax.all_gather(unembed, 'req', axis=0, tiled=True)  87.4 us
    all_gather x1, waiting for transfers between devices, on_device(): lax.all_gather(hidden, 'voc', axis=0, tiled=True)  46.9 us
    all_gather x1, blocking collectives, on_device(): lax.all_gather(targets, 'voc', axis=0, tiled=True)  16.5 us
    dot_general x4, matrix products, on_device(): lax.dot_general(normed, piece, (((1,), (1,)), ((), ())), preferred_elemen...  10.6 us
  transfers between devices with their start and end apart: 2, of which 2 were waited for; matrix products, arithmetic and copies ran while one was open for 1% of the time, Pallas kernels for 0%

commit v1 on v0

--- a/solution.py
+++ b/solution.py
@@ -25,7 +25,9 @@
 
 def on_device(hidden, norm_gain, unembed, targets, live):
     rows, wanted = (
-        lax.all_gather(hidden, "voc", axis=0, tiled=True),
+        jnp.concatenate(
+            lax.all_to_all(jnp.stack([hidden] * lax.axis_size("voc")), "voc", 0, 0), axis=0
+        ),
         lax.all_gather(targets, "voc", axis=0, tiled=True),
     )
     wide = rows.astype(jnp.float32)

time: 284 us -> 227 us (0.80)
  the two profiles are of different devices: /device:TPU:16 before, /device:TPU:192 now
where the time goes in v1:
time: 227 us; the launch traced here: 226 us
  blocking collectives  181 us (80%)
  between operations  14.2 us (6%)
  matrix products  10.9 us (5%)
  other arithmetic  7.98 us (4%)
  starting transfers between devices  7.27 us (3%)
  local copies, waits for them, and re-layouts  4.18 us (2%)
    all_gather x4, blocking collectives, merged_2(): pieces = jax.tree.map(lambda part: lax.all_gather(part, axis), value)  97.8 us
    all_gather x1, blocking collectives, on_device(): lax.all_gather(targets, 'voc', axis=0, tiled=True)  82.9 us
    dot_general x4, matrix products, on_device(): lax.dot_general(normed, piece, (((1,), (1,)), ((), ())), preferred_elemen...  10.9 us
    all_to_all x1, starting transfers between devices, on_device(): lax.all_to_all(jnp.stack([hidden] * lax.axis_size('voc')), 'voc', 0, 0)  7.23 us
  transfers between devices with their start and end apart: 2, of which 0 were waited for; matrix products, arithmetic and copies ran while one was open for 3% of the time, Pallas kernels for 0%

profile of v1, /device:TPU:192, one launch (start us, length us, event | category | flops | bytes accessed | tf_op | source)
XLA Modules:
  0.0 226.3 jit_solution(15937294179767699793)
XLA Ops:
  7.2 0.0 all-gather.7.cloned.1.call-start
  7.2 0.7 all-gather.7.cloned.1.call-update
  7.9 3.2 %stack.2 = bf16[8,128,1600]{1,2,0:T(8,128)(2,1)} broadcast(bf16[128,1600]{0,1:T(8,128)(2,1)} %param.7), dimensions={1,2} | broadcast | bytes 3686400 | tf_op jit(solution)/shard_map/stack | solution.py:29
  11.1 7.2 %all-to-all-start = ((bf16[8,128,1600]{1,2,0:T(8,128)(2,1)}), bf16[8,128,1600]{1,2,0:T(8,128)(2,1)S(1)}, u32[]{:S(2)}, u32[]{:S(2)}) async-start(bf16[8,128,1600]{1,2,0:T(8,128)(2,1)} %stack.2), calls=%async_computation | async-start | bytes 6553600 | tf_op jit(solution)/shard_map/all_to_all | solution.py:29
  18.3 0.0 copy-done.2
  18.3 82.9 %all-gather.4 = s32[8,1,128]{2,1,0:T(1,128)S(1)} all-gather(s32[1,1,128]{2,1,0:T(1,128)S(1)} %bitcast.89), channel_id=1, replica_groups=mesh['req'=64,'voc'=8] {'voc'}, dimensions={0}, use_global_device_ids=true | all-gather | bytes 4608 | tf_op jit(solution)/shard_map/all_gather | solution.py:31
  101.2 0.0 all-to-all-done
  101.2 0.6 fusion
  101.9 0.0 copy-done.1
  101.9 2.5 %fusion.2 = bf16[1024,1600]{0,1:T(8,128)(2,1)} fusion(f32[1600]{0:T(1024)S(1)} %copy-done.1, f32[1024]{0:T(1024)S(1)} %rsqrt_bitcast_fusion, bf16[8,128,1600]{1,2,0:T(8,128)(2,1)S(1)} %all-to-all-done), kind=kLoop, calls=%fused_computation.11 | loop fusion | flops 6553600 | bytes 6564096 | tf_op jit(solution)/shard_map/convert_element_type | solution.py:36
  104.4 4.7 %fusion.40 = (f32[1024]{0:T(1024)S(1)}, f32[1024,512]{0,1:T(8,128)S(1)}) fusion(bf16[1024,1600]{0,1:T(8,128)(2,1)} %fusion.2, bf16[2048,1600]{1,0:T(8,128)(2,1)} %all-gather.7.cloned.1.call-done), kind=kOutput, calls=%fused_computation.104 | convolution fusion | flops 1678244864 | bytes 7081984 | tf_op jit(solution)/shard_map/dot_general | solution.py:48
  109.1 0.7 copy-done.4
  109.8 2.1 fusion.41
  111.9 2.1 fusion.42
  113.9 2.1 fusion.43
  116.0 0.0 copy-start.3
  116.0 3.9 %fusion.3 = (f32[1024]{0:T(1024)S(1)}, f32[1024]{0:T(1024)S(1)}, f32[1024]{0:T(1024)S(1)}, f32[1024]{0:T(1024)S(1)}, f32[1024]{0:T(1024)S(1)}, /*index=5*/f32[10...) fusion(f32[1024,512]{0,1:T(8,128)S(1)} %get-tuple-element.108, ...), kind=kLoop, calls=%fused_computation.20 | loop fusion | flops 14667776 | bytes 8466432 | tf_op jit(solution)/shard_map/reduce_sum | solution.py:57
  120.0 24.5 %all-gather = f32[8192]{0:T(1024)S(1)} all-gather(f32[1024]{0:T(1024)S(1)} %add_add_fusion), channel_id=2, replica_groups=mesh['req'=64,'voc'=8] {'voc'}, dimensions={0}, use_global_device_ids=true | all-gather | bytes 36864 | tf_op jit(solution)/shard_map/all_gather | solution.py:8
  144.4 0.1 add_bitcast_fusion
  144.6 24.5 %all-gather.1 = f32[8,1,1024]{2,1,0:T(1,128)S(1)} all-gather(f32[1,1,1024]{2,1,0:T(1,128)S(1)} %get-tuple-element.95), channel_id=1, replica_groups=mesh['req'=64,'voc'=8] {'voc'}, dimensions={0}, use_global_device_ids=true | all-gather | bytes 36864 | tf_op jit(solution)/shard_map/all_gather | solution.py:8
  169.0 24.5 %all-gather.2 = f32[8,1,1024]{2,1,0:T(1,128)S(1)} all-gather(f32[1,1,1024]{2,1,0:T(1,128)S(1)} %get-tuple-element.94), channel_id=1, replica_groups=mesh['req'=64,'voc'=8] {'voc'}, dimensions={0}, use_global_device_ids=true | all-gather | bytes 36864 | tf_op jit(solution)/shard_map/all_gather | solution.py:8
  193.5 24.5 %all-gather.3 = f32[8,1,1024]{2,1,0:T(1,128)S(1)} all-gather(f32[1,1,1024]{2,1,0:T(1,128)S(1)} %get-tuple-element.88), channel_id=1, replica_groups=mesh['req'=64,'voc'=8] {'voc'}, dimensions={0}, use_global_device_ids=true | all-gather | bytes 36864 | tf_op jit(solution)/shard_map/all_gather | solution.py:8
  218.0 0.8 while.16
  218.8 0.6 subtract_multiply_fusion
  (66 shorter events, 0.5 us)
Async XLA Ops:
  7.2 97.2 %all-gather.7.cloned.1.call-start = ((), (), s32[]{:S(2)}) async-start(), calls=%async_computation.1 | async-start | bytes 6922240 | tf_op jit(solution)/shard_map/all_gather | solution.py:43
  11.1 7.2 %copy-start.2 = (s32[128]{0:T(128)S(1)}, s32[128]{0:T(128)}, u32[]{:S(2)}) copy-start(s32[128]{0:T(128)} %param.10) | copy-start | bytes 1540
  11.1 90.1 %all-to-all-start = ((bf16[8,128,1600]{1,2,0:T(8,128)(2,1)}), bf16[8,128,1600]{1,2,0:T(8,128)(2,1)S(1)}, u32[]{:S(2)}, u32[]{:S(2)}) async-start(bf16[8,128,1600]{1,2,0:T(8,128)(2,1)} %stack.2), calls=%async_computation | async-start | bytes 6553600 | tf_op jit(solution)/shard_map/all_to_all | solution.py:29
  18.3 83.6 %copy-start.1 = (f32[1600]{0:T(1024)S(1)}, f32[1600]{0:T(1024)}, u32[]{:S(2)}) copy-start(f32[1600]{0:T(1024)} %param.8) | copy-start | bytes 19204
  104.4 4.7 %copy-start = (bf16[1024,1600]{0,1:T(8,128)(2,1)S(1)}, bf16[1024,1600]{0,1:T(8,128)(2,1)}, u32[]{:S(2)}) copy-start(bf16[1024,1600]{0,1:T(8,128)(2,1)} %fusion.2) | copy-start | bytes 9830404
  104.4 5.4 %copy-start.4 = (bf16[2048,1600]{1,0:T(8,128)(2,1)S(1)}, bf16[2048,1600]{1,0:T(8,128)(2,1)}, u32[]{:S(2)}) copy-start(bf16[2048,1600]{1,0:T(8,128)(2,1)} %all-gather.7.cloned.1.call-done) | copy-start | bytes 19660804
  116.0 102.8 %copy-start.3 = (s32[128]{0:T(128)S(1)}, s32[128]{0:T(128)}, u32[]{:S(2)}) copy-start(s32[128]{0:T(128)} %param.11) | copy-start | bytes 1540
Sparse Core Ops, SparseCore 0:
  11.3 88.6 all-gather.6
